TPU v7x, 512 devices: a whole 4x4x16 slice. The times are simulated.
512 devices in a mesh: expert: 64 (over x, z_lo, core), shard: 8 (over z_hi, y).
Axes of the slice: x: 4, y: 4, z: 16 (z_hi: 2, z_lo: 8; z = z_hi * 8 + z_lo), core: 2. Of those that a mesh axis runs over, the one named last changes fastest.
Arguments:
- tokens: bfloat16 [2560, 4096], P('expert'), may hold values from -6 to 6
- expert_ids: int32 [2560, 8], P('expert'), may hold values from 0 to 63, all different within a row; in each aligned block of 40 rows (0 to 39, 40 to 79, ...) at most 10 rows name the same one
- route_weights: float32 [2560, 8], P('expert'), may hold values from 0.05 to 0.5
- partner: int32 [64], replicated, may hold values from 0 to 63, as said below
- gate_up: bfloat16 [64, 2, 768, 4096], P('expert', None, 'shard'), may hold values from -0.09375 to 0.09375
- down_weight: bfloat16 [64, 768, 4096], P('expert', None, 'shard'), may hold values from -0.21875 to 0.21875
- down_grad: bfloat16 [64, 128, 4096], P('expert', None, 'shard'), may hold values from -6 to 6
- moment_one: float32 [64, 128, 4096], P('expert', None, 'shard'), may hold values from -6 to 6
- moment_two: float32 [64, 128, 4096], P('expert', None, 'shard'), may hold values from 0.3 to 3
Outputs:
- combined: bfloat16 [2560, 4096], P('expert', 'shard')
- trained_rows: bfloat16 [64, 128, 4096], P('expert', None, 'shard')
- first_moment: float32 [64, 128, 4096], P('expert', None, 'shard')
- second_moment: float32 [64, 128, 4096], P('expert', None, 'shard')
Inputs may be any that keep to these rules, and one draw needn't show every extreme that they name: `expert_ids`: each row names 8 different experts. In each aligned block of 40 rows (the rows held by one index of expert) no expert is named by more than 10 rows, a bound that some block reaches. partner[partner[p]] = p and partner[p] != p for every p: the list splits all 64 indices into pairs.
All inputs are finite; a program needn't handle non-finite values.
Results may differ from a plain program's by a relative error of at most 0.0058.
Values may be sent and summed in bfloat16 or wider, within the bound.
No kernel may reach another device: no remote copies, remote signals or barrier semaphores. Data moves between devices by JAX's collectives and lax.ppermute only.
A program may use at most 64 MiB of HBM per device.

v0:
```python
import jax
import jax.numpy as jnp
from jax import lax
from jax.sharding import PartitionSpec as P

STEP = 100


learn_rate = 0.01
beta_one = 0.9
beta_two = 0.999
epsilon = 1e-08
decay_rate = 0.1


def adamw(weight, gradient, first, second):
    grad_wide = gradient.astype(jnp.float32)
    first_new = beta_one * first + (1.0 - beta_one) * grad_wide
    second_new = beta_two * second + (1.0 - beta_two) * grad_wide * grad_wide
    first_hat = first_new / (1.0 - beta_one**STEP)
    second_hat = second_new / (1.0 - beta_two**STEP)
    weight_wide = weight.astype(jnp.float32)
    updated = weight_wide - learn_rate * (
        first_hat / (jnp.sqrt(second_hat) + epsilon) + decay_rate * weight_wide
    )
    return (updated.astype(jnp.bfloat16), first_new, second_new)


def relocate(payload, first, second, partner):
    spread = (
        lax.all_to_all(payload, "expert", split_axis=0, concat_axis=0, tiled=True),
        lax.all_to_all(
            first.astype(jnp.bfloat16), "expert", split_axis=0, concat_axis=0, tiled=True
        ).astype(first.dtype),
        lax.all_to_all(
            second.astype(jnp.bfloat16), "expert", split_axis=0, concat_axis=0, tiled=True
        ).astype(second.dtype),
    )
    return (
        lax.all_to_all(
            jnp.take(spread[0], partner, axis=0), "expert", split_axis=0, concat_axis=0, tiled=True
        ),
        lax.all_to_all(
            jnp.take(spread[1], partner, axis=0).astype(jnp.bfloat16),
            "expert",
            split_axis=0,
            concat_axis=0,
            tiled=True,
        ).astype(jnp.float32),
        lax.all_to_all(
            jnp.take(spread[2], partner, axis=0).astype(jnp.bfloat16),
            "expert",
            split_axis=0,
            concat_axis=0,
            tiled=True,
        ).astype(jnp.float32),
    )


def shards(
    tokens,
    expert_ids,
    route_weights,
    partner,
    gate_up,
    down_weight,
    down_grad,
    moment_one,
    moment_two,
):
    groups = lax.axis_size("expert")
    token_count = tokens.shape[0]
    model_width = tokens.shape[1]
    part_width = down_weight.shape[2]
    trained = down_grad.shape[1]
    capacity = 2 * token_count * expert_ids.shape[1] // groups
    new_rows, first_new, second_new = adamw(
        down_weight[:, :trained], down_grad, moment_one, moment_two
    )
    down_new = jnp.concatenate([new_rows, down_weight[:, trained:]], axis=1)
    first_flat = first_new.reshape(groups, -1)
    second_flat = second_new.reshape(groups, -1)
    arrived = relocate(new_rows.reshape(groups, -1), first_flat, second_flat, partner)
    rows_out = arrived[0].reshape(new_rows.shape)
    first_out = arrived[1].reshape(first_new.shape)
    second_out = arrived[2].reshape(second_new.shape)
    experts = jnp.arange(groups, dtype=jnp.int32)
    picked = (expert_ids[:, :, None] == experts[None, None, :]).astype(jnp.int32)
    running = jnp.cumsum(picked.reshape(-1, groups), axis=0).reshape(picked.shape)
    slot_index = jnp.sum((running - 1) * picked, axis=2)
    position = expert_ids * capacity + slot_index
    positions = jnp.arange(groups * capacity, dtype=jnp.int32)
    matches = position[None, :, :] == positions[:, None, None]
    dispatch = jnp.sum(matches.astype(jnp.int32), axis=2).astype(jnp.bfloat16)
    weighting = jnp.sum(jnp.where(matches, route_weights[None, :, :], 0.0), axis=2)
    outgoing = jnp.dot(dispatch, tokens, preferred_element_type=jnp.float32).astype(jnp.bfloat16)
    outgoing = outgoing.reshape(groups, capacity, tokens.shape[1])
    joined = gate_up.reshape(-1, model_width)
    hidden_count = joined.shape[0] // 2
    down_rows = down_new.reshape(-1, part_width)
    received = lax.all_to_all(outgoing, "expert", split_axis=0, concat_axis=0, tiled=True)
    leading = received.shape[:2]
    token_rows = received.reshape(-1, model_width)
    projected = lax.dot_general(
        token_rows, joined, (((1,), (1,)), ((), ())), preferred_element_type=jnp.float32
    )
    hidden = (jax.nn.silu(projected[:, :hidden_count]) * projected[:, hidden_count:]).astype(
        jnp.bfloat16
    )
    summed = jnp.dot(
        lax.all_gather(hidden, "shard", axis=1, tiled=True),
        down_rows,
        preferred_element_type=jnp.float32,
    )
    results = summed.astype(jnp.bfloat16).reshape(leading + (part_width,))
    returned = lax.all_to_all(results, "expert", split_axis=0, concat_axis=0, tiled=True)
    returned_wide = returned.reshape(-1, part_width).astype(jnp.float32)
    combined = jnp.dot(
        weighting.T,
        returned_wide,
        precision=lax.Precision.HIGHEST,
        preferred_element_type=jnp.float32,
    ).astype(jnp.bfloat16)
    return (combined, rows_out, first_out, second_out)


def solution(mesh):
    return jax.shard_map(
        shards,
        mesh=mesh,
        in_specs=(
            P("expert", None),
            P("expert", None),
            P("expert", None),
            P(),
            P("expert", None, "shard", None),
            P("expert", None, "shard"),
            P("expert", None, "shard"),
            P("expert", None, "shard"),
            P("expert", None, "shard"),
        ),
        out_specs=(
            P("expert", "shard"),
            P("expert", None, "shard"),
            P("expert", None, "shard"),
            P("expert", None, "shard"),
        ),
        check_vma=False,
    )
```

profile of v0, /device:TPU:1, one launch (start us, length us, event | category | flops | bytes accessed | tf_op | source)
XLA Modules:
  0.0 654.9 jit_solution(1038525018546543560)
XLA Ops:
  0.7 1.5 fusion.9
  2.2 0.5 broadcast.77
  2.8 1.4 reduce.8
  4.1 0.7 reshape.201
  4.9 17.0 %all-to-all-start.2 = ((bf16[64,2,512]{2,1,0:T(2,128)(2,1)}), bf16[64,2,512]{2,1,0:T(2,128)(2,1)S(1)}, u32[]{:S(2)}, u32[]{:S(2)}) async-start(bf16[64,2,512]{2,1,0:T(2,128)(2,1)} %reshape.201), calls=%async_computation.2 | async-start | bytes 262144 | tf_op jit(solution)/shard_map/all_to_all | solution.py:31
  21.9 0.8 copy.43
  22.8 1.4 reduce.10
  24.2 0.7 reshape.209
  25.0 11.5 %all-to-all-done.2 = bf16[64,2,512]{2,1,0:T(2,128)(2,1)S(1)} async-done(((bf16[64,2,512]{2,1,0:T(2,128)(2,1)}), bf16[64,2,512]{2,1,0:T(2,128)(2,1)S(1)}, u32[]{:S(2)}, u32[]{:S(2)}) %all-to-all-start.2) | async-done | bytes 131104 | tf_op jit(solution)/shard_map/all_to_all | solution.py:31
  36.5 6.1 all-to-all-start.6
  42.5 0.9 reduce-window.6
  44.0 1.4 reduce.11
  45.4 0.7 reshape.205
  46.1 10.9 %all-to-all-done.6 = bf16[64,2,512]{2,1,0:T(2,128)(2,1)S(1)} async-done(((bf16[64,2,512]{2,1,0:T(2,128)(2,1)}), bf16[64,2,512]{2,1,0:T(2,128)(2,1)S(1)}, u32[]{:S(2)}, u32[]{:S(2)}) %all-to-all-start.6) | async-done | bytes 131104 | tf_op jit(solution)/shard_map/all_to_all | solution.py:35
  57.1 6.1 all-to-all-start.4
  63.5 3.9 convolution_convert_fusion
  67.3 8.2 %reshape.154 = bf16[64,10,4096]{2,1,0:T(8,128)(2,1)} reshape(bf16[640,4096]{1,0:T(8,128)(2,1)} %convolution_convert_fusion) | data formatting | bytes 10485760 | tf_op jit(solution)/shard_map/reshape | solution.py:97
  75.6 2.1 all-to-all-done.4
  77.7 11.3 %all-to-all-start = ((bf16[64,10,4096]{2,1,0:T(8,128)(2,1)}), bf16[64,10,4096]{2,1,0:T(8,128)(2,1)}, u32[]{:S(2)}, u32[]{:S(2)}) async-start(bf16[64,10,4096]{2,1,0:T(8,128)(2,1)} %reshape.154), calls=%async_computation | async-start | bytes 16777216 | tf_op jit(solution)/shard_map/all_to_all | solution.py:101
  89.2 0.7 gather_fusion
  90.0 0.7 reduce.9
  90.7 0.7 reshape.203
  91.4 363.9 %all-to-all-done = bf16[64,10,4096]{2,1,0:T(8,128)(2,1)} async-done(((bf16[64,10,4096]{2,1,0:T(8,128)(2,1)}), bf16[64,10,4096]{2,1,0:T(8,128)(2,1)}, u32[]{:S(2)}, u32[]{:S(2)}) %all-to-all-start) | async-done | bytes 5242912 | tf_op jit(solution)/shard_map/all_to_all | solution.py:101
  455.3 7.8 %all-to-all-start.3 = ((bf16[64,2,512]{2,1,0:T(2,128)(2,1)}), bf16[64,2,512]{2,1,0:T(2,128)(2,1)S(1)}, u32[]{:S(2)}, u32[]{:S(2)}) async-start(bf16[64,2,512]{2,1,0:T(2,128)(2,1)} %reshape.203), calls=%async_computation.3 | async-start | bytes 262144 | tf_op jit(solution)/shard_map/all_to_all | solution.py:40
  463.2 0.7 gather_fusion.2
  464.1 0.7 gather_fusion.1
  464.9 0.7 reduce.12
  465.6 0.7 reshape.207
  466.3 0.7 reduce.13
  467.0 0.7 reshape.211
  467.7 8.6 %reshape.155 = bf16[640,4096]{1,0:T(8,128)(2,1)} reshape(bf16[64,10,4096]{2,1,0:T(8,128)(2,1)} %all-to-all-done) | data formatting | bytes 10485760 | tf_op jit(solution)/shard_map/reshape | solution.py:103
  476.3 1.3 all-to-all-done.3
  477.6 11.9 %all-to-all-start.5 = ((bf16[64,2,512]{2,1,0:T(2,128)(2,1)}), bf16[64,2,512]{2,1,0:T(2,128)(2,1)S(1)}, u32[]{:S(2)}, u32[]{:S(2)}) async-start(bf16[64,2,512]{2,1,0:T(2,128)(2,1)} %reshape.207), calls=%async_computation.5 | async-start | bytes 262144 | tf_op jit(solution)/shard_map/all_to_all | solution.py:43
  489.5 4.4 fusion.16
  494.0 10.1 %all-to-all-done.5 = bf16[64,2,512]{2,1,0:T(2,128)(2,1)S(1)} async-done(((bf16[64,2,512]{2,1,0:T(2,128)(2,1)}), bf16[64,2,512]{2,1,0:T(2,128)(2,1)S(1)}, u32[]{:S(2)}, u32[]{:S(2)}) %all-to-all-start.5) | async-done | bytes 131104 | tf_op jit(solution)/shard_map/all_to_all | solution.py:43
  504.1 6.1 all-to-all-start.7
  510.1 69.2 %all_gather.3 = bf16[640,768]{0,1:T(8,128)(2,1)S(1)} all-gather(bf16[640,96]{0,1:T(8,128)(2,1)S(1)} %fusion.7), channel_id=1, replica_groups=mesh['expert'=64,'shard'=8] {'shard'}, dimensions={1}, use_global_device_ids=true | all-gather | bytes 1105920 | tf_op jit(solution)/shard_map/all_gather | solution.py:111
  579.3 0.7 convolution_convert_fusion.1
  580.0 1.2 reshape.158
  581.2 21.1 %all-to-all-start.1 = ((bf16[64,10,512]{2,1,0:T(8,128)(2,1)}), bf16[64,10,512]{2,1,0:T(8,128)(2,1)S(1)}, u32[]{:S(2)}, u32[]{:S(2)}) async-start(bf16[64,10,512]{2,1,0:T(8,128)(2,1)} %reshape.158), calls=%async_computation.1 | async-start | bytes 2097152 | tf_op jit(solution)/shard_map/all_to_all | solution.py:116
  602.8 0.7 reduce.2
  603.6 0.7 reshape.160
  604.4 0.7 convert_reduce_fusion.2
  605.1 0.7 reshape.163
  605.9 0.7 convert_reduce_fusion.1
  606.7 0.7 reshape.165
  607.4 46.2 %all-to-all-done.1 = bf16[64,10,512]{2,1,0:T(8,128)(2,1)S(1)} async-done(((bf16[64,10,512]{2,1,0:T(8,128)(2,1)}), bf16[64,10,512]{2,1,0:T(8,128)(2,1)S(1)}, u32[]{:S(2)}, u32[]{:S(2)}) %all-to-all-start.1) | async-done | bytes 655392 | tf_op jit(solution)/shard_map/all_to_all | solution.py:116
  653.8 1.0 convolution_convert_fusion.2
  (42 shorter events, 2.8 us)
Async XLA Ops:
  0.6 488.9 %copy-start = (bf16[1,2,96,4096]{3,2,1,0:T(8,128)(2,1)S(1)}, bf16[1,2,96,4096]{3,2,1,0:T(8,128)(2,1)}, u32[]{:S(2)}) copy-start(bf16[1,2,96,4096]{3,2,1,0:T(8,128)(2,1)} %param.15) | copy-start | bytes 4718596
  0.6 62.8 %copy-start.1 = (bf16[40,4096]{1,0:T(8,128)(2,1)S(1)}, bf16[40,4096]{1,0:T(8,128)(2,1)}, u32[]{:S(2)}) copy-start(bf16[40,4096]{1,0:T(8,128)(2,1)} %param.11) | copy-start | bytes 983044
  4.9 31.6 %all-to-all-start.2 = ((bf16[64,2,512]{2,1,0:T(2,128)(2,1)}), bf16[64,2,512]{2,1,0:T(2,128)(2,1)S(1)}, u32[]{:S(2)}, u32[]{:S(2)}) async-start(bf16[64,2,512]{2,1,0:T(2,128)(2,1)} %reshape.201), calls=%async_computation.2 | async-start | bytes 262144 | tf_op jit(solution)/shard_map/all_to_all | solution.py:31
  36.5 20.6 %all-to-all-start.6 = ((bf16[64,2,512]{2,1,0:T(2,128)(2,1)}), bf16[64,2,512]{2,1,0:T(2,128)(2,1)S(1)}, u32[]{:S(2)}, u32[]{:S(2)}) async-start(bf16[64,2,512]{2,1,0:T(2,128)(2,1)} %reshape.209), calls=%async_computation.6 | async-start | bytes 262144 | tf_op jit(solution)/shard_map/all_to_all | solution.py:35
  57.1 20.6 %all-to-all-start.4 = ((bf16[64,2,512]{2,1,0:T(2,128)(2,1)}), bf16[64,2,512]{2,1,0:T(2,128)(2,1)S(1)}, u32[]{:S(2)}, u32[]{:S(2)}) async-start(bf16[64,2,512]{2,1,0:T(2,128)(2,1)} %reshape.205), calls=%async_computation.4 | async-start | bytes 262144 | tf_op jit(solution)/shard_map/all_to_all | solution.py:32
  75.6 13.4 %copy-start.3 = (s32[64]{0:T(128)S(1)}, s32[64]{0:T(128)}, u32[]{:S(2)}) copy-start(s32[64]{0:T(128)} %param.14) | copy-start | bytes 772
  77.7 377.6 %all-to-all-start = ((bf16[64,10,4096]{2,1,0:T(8,128)(2,1)}), bf16[64,10,4096]{2,1,0:T(8,128)(2,1)}, u32[]{:S(2)}, u32[]{:S(2)}) async-start(bf16[64,10,4096]{2,1,0:T(8,128)(2,1)} %reshape.154), calls=%async_computation | async-start | bytes 16777216 | tf_op jit(solution)/shard_map/all_to_all | solution.py:101
  455.3 22.3 %all-to-all-start.3 = ((bf16[64,2,512]{2,1,0:T(2,128)(2,1)}), bf16[64,2,512]{2,1,0:T(2,128)(2,1)S(1)}, u32[]{:S(2)}, u32[]{:S(2)}) async-start(bf16[64,2,512]{2,1,0:T(2,128)(2,1)} %reshape.203), calls=%async_computation.3 | async-start | bytes 262144 | tf_op jit(solution)/shard_map/all_to_all | solution.py:40
  476.3 103.0 %slice-start = ((bf16[1,768,512]{2,1,0:T(8,128)(2,1)}), bf16[1,640,512]{2,1,0:T(8,128)(2,1)S(1)}, s32[]{:S(2)}) async-start(bf16[1,768,512]{2,1,0:T(8,128)(2,1)} %param.16), calls=%async_computation.8 | async-start | bytes 1310720 | tf_op jit(solution)/shard_map/slice | solution.py:80
  477.6 26.5 %all-to-all-start.5 = ((bf16[64,2,512]{2,1,0:T(2,128)(2,1)}), bf16[64,2,512]{2,1,0:T(2,128)(2,1)S(1)}, u32[]{:S(2)}, u32[]{:S(2)}) async-start(bf16[64,2,512]{2,1,0:T(2,128)(2,1)} %reshape.207), calls=%async_computation.5 | async-start | bytes 262144 | tf_op jit(solution)/shard_map/all_to_all | solution.py:43
  493.9 108.4 %copy-start.2 = (f32[40,8]{0,1:T(8,128)S(1)}, f32[40,8]{0,1:T(8,128)}, u32[]{:S(2)}) copy-start(f32[40,8]{0,1:T(8,128)} %param.13) | copy-start | bytes 3844
  504.1 77.1 %all-to-all-start.7 = ((bf16[64,2,512]{2,1,0:T(2,128)(2,1)}), bf16[64,2,512]{2,1,0:T(2,128)(2,1)S(1)}, u32[]{:S(2)}, u32[]{:S(2)}) async-start(bf16[64,2,512]{2,1,0:T(2,128)(2,1)} %reshape.211), calls=%async_computation.7 | async-start | bytes 262144 | tf_op jit(solution)/shard_map/all_to_all | solution.py:50
  581.2 72.4 %all-to-all-start.1 = ((bf16[64,10,512]{2,1,0:T(8,128)(2,1)}), bf16[64,10,512]{2,1,0:T(8,128)(2,1)S(1)}, u32[]{:S(2)}, u32[]{:S(2)}) async-start(bf16[64,10,512]{2,1,0:T(8,128)(2,1)} %reshape.158), calls=%async_computation.1 | async-start | bytes 2097152 | tf_op jit(solution)/shard_map/all_to_all | solution.py:116
where the time goes:
time: 656 us; the launch traced here: 655 us
  waiting for transfers between devices  446 us (68%)
  starting transfers between devices  87.3 us (13%)
  blocking collectives  69.2 us (11%)
  local copies, waits for them, and re-layouts  29.7 us (5%)
  other arithmetic  11.9 us (2%)
  matrix products  9.95 us (2%)
    all_to_all x1, waiting for transfers between devices, shards(): lax.all_to_all(outgoing, 'expert', split_axis=0, concat_axis=0, tiled=True)  364 us
    all_gather x1, blocking collectives, shards(): lax.all_gather(hidden, 'shard', axis=1, tiled=True)  69.2 us
    all_to_all x1, waiting for transfers between devices, shards(): lax.all_to_all(results, 'expert', split_axis=0, concat_axis=0, tiled=True)  46.2 us
    all_to_all x1, starting transfers between devices, shards(): lax.all_to_all(results, 'expert', split_axis=0, concat_axis=0, tiled=True)  21.1 us
    all_to_all x1, starting transfers between devices, relocate(): lax.all_to_all(payload, 'expert', split_axis=0, concat_axis=0, tiled=True)  17 us
  transfers between devices with their start and end apart: 8, of which 7 were waited for; matrix products, arithmetic and copies ran while one was open for 7% of the time, Pallas kernels for 0%

commit v1 on v0

v1 whole, which is shorter than its diff:
```python
import jax
import jax.numpy as jnp
from jax import lax
from jax.sharding import Mesh, PartitionSpec as P

STEP = 100


learn_rate = 0.01
beta_one = 0.9
beta_two = 0.999
epsilon = 1e-08
decay_rate = 0.1


def adamw(weight, gradient, first, second):
    grad_wide = gradient.astype(jnp.float32)
    first_new = beta_one * first + (1.0 - beta_one) * grad_wide
    second_new = beta_two * second + (1.0 - beta_two) * grad_wide * grad_wide
    first_hat = first_new / (1.0 - beta_one**STEP)
    second_hat = second_new / (1.0 - beta_two**STEP)
    weight_wide = weight.astype(jnp.float32)
    updated = weight_wide - learn_rate * (
        first_hat / (jnp.sqrt(second_hat) + epsilon) + decay_rate * weight_wide
    )
    return (updated.astype(jnp.bfloat16), first_new, second_new)


def relocate(rows, first, second, partner, groups):
    parts = (
        rows.reshape(groups, -1),
        first.astype(jnp.bfloat16).reshape(groups, -1),
        second.astype(jnp.bfloat16).reshape(groups, -1),
    )
    widths = [p.shape[1] for p in parts]
    payload = jnp.concatenate(parts, axis=1)
    spread = lax.all_to_all(payload, "expert", split_axis=0, concat_axis=0, tiled=True)
    back = lax.all_to_all(
        jnp.take(spread, partner, axis=0), "expert", split_axis=0, concat_axis=0, tiled=True
    )
    rows_out = back[:, : widths[0]].reshape(rows.shape)
    first_out = back[:, widths[0] : widths[0] + widths[1]].astype(jnp.float32).reshape(first.shape)
    second_out = back[:, widths[0] + widths[1] :].astype(jnp.float32).reshape(second.shape)
    return rows_out, first_out, second_out


def shards(
    tokens,
    expert_ids,
    route_weights,
    partner,
    gate_up,
    down_weight,
    down_grad,
    moment_one,
    moment_two,
):
    groups = lax.axis_size("expert")
    quarters = lax.axis_size("y")
    token_count = tokens.shape[0]
    model_width = tokens.shape[1]
    part_width = down_weight.shape[2]
    trained = down_grad.shape[1]
    capacity = 2 * token_count * expert_ids.shape[1] // groups
    quarter = model_width // quarters
    new_rows, first_new, second_new = adamw(
        down_weight[:, :trained], down_grad, moment_one, moment_two
    )
    down_new = jnp.concatenate([new_rows, down_weight[:, trained:]], axis=1)
    rows_out, first_out, second_out = relocate(new_rows, first_new, second_new, partner, groups)
    experts = jnp.arange(groups, dtype=jnp.int32)
    picked = (expert_ids[:, :, None] == experts[None, None, :]).astype(jnp.int32)
    running = jnp.cumsum(picked.reshape(-1, groups), axis=0).reshape(picked.shape)
    slot_index = jnp.sum((running - 1) * picked, axis=2)
    position = expert_ids * capacity + slot_index
    positions = jnp.arange(groups * capacity, dtype=jnp.int32)
    matches = position[None, :, :] == positions[:, None, None]
    dispatch = jnp.sum(matches.astype(jnp.int32), axis=2).astype(jnp.bfloat16)
    weighting = jnp.sum(jnp.where(matches, route_weights[None, :, :], 0.0), axis=2)
    own_quarter = lax.dynamic_slice_in_dim(tokens, lax.axis_index("y") * quarter, quarter, axis=1)
    outgoing = jnp.dot(dispatch, own_quarter, preferred_element_type=jnp.float32).astype(jnp.bfloat16)
    outgoing = outgoing.reshape(groups, capacity, quarter)
    received = lax.all_to_all(outgoing, "expert", split_axis=0, concat_axis=0, tiled=True)
    gathered = lax.all_gather(received, "y", axis=0, tiled=False)
    token_rows = gathered.reshape(quarters, groups * capacity, quarter)
    joined = gate_up.reshape(-1, quarters, quarter)
    hidden_count = joined.shape[0] // 2
    down_rows = down_new.reshape(-1, part_width)
    projected = lax.dot_general(
        token_rows, joined, (((0, 2), (1, 2)), ((), ())), preferred_element_type=jnp.float32
    )
    hidden = (jax.nn.silu(projected[:, :hidden_count]) * projected[:, hidden_count:]).astype(
        jnp.bfloat16
    )
    summed = jnp.dot(
        lax.all_gather(hidden, ("zh", "y"), axis=1, tiled=True),
        down_rows,
        preferred_element_type=jnp.float32,
    )
    results = summed.astype(jnp.bfloat16).reshape(groups, capacity, part_width)
    returned = lax.all_to_all(results, "expert", split_axis=0, concat_axis=0, tiled=True)
    returned_wide = returned.reshape(-1, part_width).astype(jnp.float32)
    combined = jnp.dot(
        weighting.T,
        returned_wide,
        precision=lax.Precision.HIGHEST,
        preferred_element_type=jnp.float32,
    ).astype(jnp.bfloat16)
    return (combined, rows_out, first_out, second_out)


def solution(mesh):
    shard_size = mesh.shape["shard"]
    quarters = 4 if shard_size % 4 == 0 else shard_size
    devices = mesh.devices.reshape(mesh.shape["expert"], shard_size // quarters, quarters)
    split_mesh = Mesh(devices, ("expert", "zh", "y"))
    sh = ("zh", "y")
    return jax.shard_map(
        shards,
        mesh=split_mesh,
        in_specs=(
            P("expert", None),
            P("expert", None),
            P("expert", None),
            P(),
            P("expert", None, sh, None),
            P("expert", None, sh),
            P("expert", None, sh),
            P("expert", None, sh),
            P("expert", None, sh),
        ),
        out_specs=(
            P("expert", sh),
            P("expert", None, sh),
            P("expert", None, sh),
            P("expert", None, sh),
        ),
        check_vma=False,
    )
```

time: 656 us -> 376 us (0.57)
  waiting for transfers between devices: 446 us -> 83 us
  blocking collectives: 69.2 us -> 186 us
  starting transfers between devices: 87.3 us -> 42.2 us
  between operations: 1.01 us -> 14.4 us
  other arithmetic: 11.9 us -> 4.02 us
  local copies, waits for them, and re-layouts: 29.7 us -> 37.4 us
    all_to_all x6 -> x1, waiting for transfers between devices: 388 us -> 0.01 us  [relocate(): lax.all_to_all(jnp.take(spread, partner, axis=0), 'expert', split_axis=0,...]
    all_to_all x0 -> x1, blocking collectives: none -> 113 us  [shards(): lax.all_to_all(outgoing, 'expert', split_axis=0, concat_axis=0, tiled=True)]
    all_to_all x6 -> x1, starting transfers between devices: 49.2 us -> 7.46 us  [relocate(): lax.all_to_all(jnp.take(spread, partner, axis=0), 'expert', split_axis=0,...]
    all_gather x0 -> x1, waiting for transfers between devices: none -> 13 us  [shards(): gathered = lax.all_gather(received, 'y', axis=0, tiled=False)]
    all_to_all x1, waiting for transfers between devices: 11.5 us -> 24.3 us  [relocate(): lax.all_to_all(payload, 'expert', split_axis=0, concat_axis=0, tiled=True)]
    all_gather x0 -> x1, local copies, waits for them, and re-layouts: none -> 9.08 us  [shards(): gathered = lax.all_gather(received, 'y', axis=0, tiled=False)]
    all_to_all x1, starting transfers between devices: 17 us -> 8.43 us  [relocate(): lax.all_to_all(payload, 'expert', split_axis=0, concat_axis=0, tiled=True)]
    reshape x4 -> x10, local copies, waits for them, and re-layouts: 18.7 us -> 17.8 us  [the longest x1 10.7 us: shards(): token_rows = gathered.reshape(quarters, groups * capacity, quarter)]
  transfers between devices with their start and end apart: 8 -> 4, of which waited for: 7 -> 3; matrix products, arithmetic and copies ran while one was open for 7% -> 10% of each run, Pallas kernels for 0% -> 0%
where the time goes in v1:
time: 376 us
  blocking collectives  186 us (49%)
  waiting for transfers between devices  83 us (22%)
  starting transfers between devices  42.2 us (11%)
  local copies, waits for them, and re-layouts  37.4 us (10%)
  between operations  14.4 us (4%)
  matrix products  8.05 us (2%)
  other arithmetic  4.02 us (1%)
    all_to_all x1, blocking collectives, shards(): lax.all_to_all(outgoing, 'expert', split_axis=0, concat_axis=0, tiled=True)  113 us
    all_gather x1, blocking collectives, shards(): lax.all_gather(hidden, ('zh', 'y'), axis=1, tiled=True)  73.6 us
    all_to_all x1, waiting for transfers between devices, shards(): lax.all_to_all(results, 'expert', split_axis=0, concat_axis=0, tiled=True)  45.7 us
    all_to_all x1, starting transfers between devices, shards(): lax.all_to_all(results, 'expert', split_axis=0, concat_axis=0, tiled=True)  26.3 us
    all_to_all x1, waiting for transfers between devices, relocate(): lax.all_to_all(payload, 'expert', split_axis=0, concat_axis=0, tiled=True)  24.3 us
    all_gather x1, waiting for transfers between devices, shards(): gathered = lax.all_gather(received, 'y', axis=0, tiled=False)  13 us
    reshape x1, local copies, waits for them, and re-layouts, shards(): token_rows = gathered.reshape(quarters, groups * capacity, quarter)  10.7 us
    all_gather x1, local copies, waits for them, and re-layouts, shards(): gathered = lax.all_gather(received, 'y', axis=0, tiled=False)  9.08 us
  transfers between devices with their start and end apart: 4, of which 3 were waited for; matrix products, arithmetic and copies ran while one was open for 10% of the time, Pallas kernels for 0%

profile of v1, /device:TPU:1, one launch (start us, length us, event | category | flops | bytes accessed | tf_op | source)
XLA Modules:
  0.0 375.5 jit_solution(12620544177419699201)
XLA Ops:
  7.2 0.0 copy-start
  7.2 0.0 all-gather.3.cloned.1.call-start
  7.2 0.8 copy.41
  8.0 0.1 eq.37
  8.2 0.9 reduce-window.6
  9.1 0.2 slice_reduce_fusion
  9.3 0.1 bitcast_bitcast_fusion
  9.5 0.1 reduce_sum.30
  9.6 0.3 convert_reduce_fusion
  9.9 1.6 convolution_convert_fusion
  11.5 2.4 reshape.105
  13.9 112.8 %all_to_all.31 = bf16[64,10,1024]{2,1,0:T(8,128)(2,1)S(1)} all-to-all(bf16[64,10,1024]{2,1,0:T(8,128)(2,1)S(1)} %reshape.105), channel_id=1, replica_groups=mesh['expert'=64,'zh'=2,'y'=4] {'expert'}, dimensions={0} | all-to-all | bytes 2621440 | tf_op jit(solution)/shard_map/all_to_all | solution.py:83
  126.7 1.8 copy.46
  128.4 0.0 all-gather.3.cloned.1.call-update
  128.5 0.3 fusion.13
  128.9 0.5 copy-done.3
  129.5 0.5 broadcast.67
  130.0 0.9 reduce.3
  130.9 1.0 reshape.139
  131.9 8.4 %all-to-all-start.2 = ((bf16[64,2,1536]{2,1,0:T(2,128)(2,1)}), bf16[64,2,1536]{2,1,0:T(2,128)(2,1)S(1)}, u32[]{:S(2)}, u32[]{:S(2)}) async-start(bf16[64,2,1536]{2,1,0:T(2,128)(2,1)} %reshape.139), calls=%async_computation.2 | async-start | bytes 786432 | tf_op jit(solution)/shard_map/all_to_all | solution.py:37
  140.4 24.3 %all-to-all-done.2 = bf16[64,2,1536]{2,1,0:T(2,128)(2,1)S(1)} async-done(((bf16[64,2,1536]{2,1,0:T(2,128)(2,1)}), bf16[64,2,1536]{2,1,0:T(2,128)(2,1)S(1)}, u32[]{:S(2)}, u32[]{:S(2)}) %all-to-all-start.2) | async-done | bytes 393248 | tf_op jit(solution)/shard_map/all_to_all | solution.py:37
  164.7 0.3 reshape.140
  165.0 0.1 copy.64
  165.1 0.8 gather_fusion
  165.9 0.1 bitcast_select_fusion
  166.1 0.9 reduce.4
  166.9 1.0 reshape.141
  168.0 7.5 %all-to-all-start.3 = ((bf16[64,2,1536]{2,1,0:T(2,128)(2,1)}), bf16[64,2,1536]{2,1,0:T(2,128)(2,1)}, u32[]{:S(2)}, u32[]{:S(2)}) async-start(bf16[64,2,1536]{2,1,0:T(2,128)(2,1)} %reshape.141), calls=%async_computation.3 | async-start | bytes 786432 | tf_op jit(solution)/shard_map/all_to_all | solution.py:38
  175.5 1.2 reshape.107
  176.7 13.0 %all-gather.3.cloned.1.call-done = bf16[256,10,1024]{2,0,1:T(8,128)(2,1)} async-done(((bf16[64,10,1024]{2,0,1:T(8,128)(2,1)}), bf16[256,10,1024]{2,0,1:T(8,128)(2,1)}) %all-gather.3.cloned.1.call-update) | async-done | bytes 5242896 | tf_op jit(solution)/shard_map/all_gather | solution.py:84
  189.6 9.1 %copy.47 = bf16[256,10,1024]{2,1,0:T(8,128)(2,1)} copy(bf16[256,10,1024]{2,0,1:T(8,128)(2,1)} %all-gather.3.cloned.1.call-done) | data formatting | bytes 10485760 | tf_op jit(solution)/shard_map/all_gather | solution.py:84
  198.7 10.7 %reshape.106 = bf16[4,640,1024]{2,1,0:T(8,128)(2,1)} reshape(bf16[256,10,1024]{2,1,0:T(8,128)(2,1)} %copy.47) | data formatting | bytes 10485760 | tf_op jit(solution)/shard_map/reshape | solution.py:85
  209.4 4.7 %fusion.2 = f32[640,192]{0,1:T(8,128)S(1)} fusion(bf16[4,640,1024]{2,1,0:T(8,128)(2,1)} %reshape.106, bf16[192,4,1024]{2,1,0:T(4,128)(2,1)S(1)} %reshape.107), kind=kOutput, calls=%fused_computation.5 | convolution fusion | flops 1006632960 | bytes 7307264 | tf_op jit(solution)/shard_map/dot_general | solution.py:89
  214.2 0.1 fusion.12
  214.3 73.6 %all_gather.11 = bf16[640,768]{0,1:T(8,128)(2,1)S(1)} all-gather(bf16[640,96]{0,1:T(8,128)(2,1)S(1)} %fusion.12), channel_id=1, replica_groups=mesh['expert'=64,'zh'=2,'y'=4] {'zh','y'}, dimensions={1}, use_global_device_ids=true | all-gather | bytes 1105920 | tf_op jit(solution)/shard_map/all_gather | solution.py:96
  287.9 0.7 convolution_convert_fusion.1
  288.6 1.2 reshape.109
  289.8 26.3 %all-to-all-start.1 = ((bf16[64,10,512]{2,1,0:T(8,128)(2,1)}), bf16[64,10,512]{2,1,0:T(8,128)(2,1)S(1)}, u32[]{:S(2)}, u32[]{:S(2)}) async-start(bf16[64,10,512]{2,1,0:T(8,128)(2,1)} %reshape.109), calls=%async_computation.1 | async-start | bytes 2097152 | tf_op jit(solution)/shard_map/all_to_all | solution.py:101
  316.1 0.1 copy.45
  316.2 0.3 select_reduce_fusion
  316.5 2.7 reshape.142
  319.3 0.1 copy.63
  319.5 0.7 reshape.121
  320.2 0.7 reshape.123
  320.9 0.7 reshape.114
  321.6 45.7 %all-to-all-done.1 = bf16[64,10,512]{2,1,0:T(8,128)(2,1)S(1)} async-done(((bf16[64,10,512]{2,1,0:T(8,128)(2,1)}), bf16[64,10,512]{2,1,0:T(8,128)(2,1)S(1)}, u32[]{:S(2)}, u32[]{:S(2)}) %all-to-all-start.1) | async-done | bytes 655392 | tf_op jit(solution)/shard_map/all_to_all | solution.py:101
  367.4 0.2 reshape.110
  367.6 1.0 convolution_convert_fusion.2
  (34 shorter events, 0.4 us)
Async XLA Ops:
  7.2 2.7 copy-start
  7.2 182.4 %all-gather.3.cloned.1.call-start = ((), (), s32[]{:S(2)}) async-start(), calls=%async_computation.4 | async-start | bytes 6553600 | tf_op jit(solution)/shard_map/all_gather | solution.py:84
  126.6 1.8 copy-start.2
  126.6 1.8 copy-start.5
  126.6 1.8 copy-start.6
  126.7 1.8 copy-start.7
  128.8 0.7 copy-start.3
  129.5 10.9 %copy-start.9 = (s32[64]{0:T(128)S(1)}, s32[64]{0:T(128)}, u32[]{:S(2)}) copy-start(s32[64]{0:T(128)} %param.12) | copy-start | bytes 772
  131.9 32.7 %all-to-all-start.2 = ((bf16[64,2,1536]{2,1,0:T(2,128)(2,1)}), bf16[64,2,1536]{2,1,0:T(2,128)(2,1)S(1)}, u32[]{:S(2)}, u32[]{:S(2)}) async-start(bf16[64,2,1536]{2,1,0:T(2,128)(2,1)} %reshape.139), calls=%async_computation.2 | async-start | bytes 786432 | tf_op jit(solution)/shard_map/all_to_all | solution.py:37
  166.9 8.5 %copy-start.1 = (bf16[1,2,96,4096]{3,2,1,0:T(8,128)(2,1)S(1)}, bf16[1,2,96,4096]{3,2,1,0:T(8,128)(2,1)}, u32[]{:S(2)}) copy-start(bf16[1,2,96,4096]{3,2,1,0:T(8,128)(2,1)} %param.13) | copy-start | bytes 4718596
  168.0 121.8 %all-to-all-start.3 = ((bf16[64,2,1536]{2,1,0:T(2,128)(2,1)}), bf16[64,2,1536]{2,1,0:T(2,128)(2,1)}, u32[]{:S(2)}, u32[]{:S(2)}) async-start(bf16[64,2,1536]{2,1,0:T(2,128)(2,1)} %reshape.141), calls=%async_computation.3 | async-start | bytes 786432 | tf_op jit(solution)/shard_map/all_to_all | solution.py:38
  214.2 73.7 %slice-start = ((bf16[1,768,512]{2,1,0:T(8,128)(2,1)}), bf16[1,640,512]{2,1,0:T(8,128)(2,1)S(1)}, s32[]{:S(2)}) async-start(bf16[1,768,512]{2,1,0:T(8,128)(2,1)} %param.14), calls=%async_computation.5 | async-start | bytes 1310720 | tf_op jit(solution)/shard_map/slice | solution.py:69
  214.2 73.7 %copy-start.4 = (bf16[1,128,512]{2,1,0:T(8,128)(2,1)S(1)}, bf16[1,128,512]{2,1,0:T(8,128)(2,1)}, u32[]{:S(2)}) copy-start(bf16[1,128,512]{2,1,0:T(8,128)(2,1)} %copy-done.3) | copy-start | bytes 393220
  288.6 27.5 %copy-start.8 = (f32[40,8]{0,1:T(8,128)S(1)}, f32[40,8]{0,1:T(8,128)}, u32[]{:S(2)}) copy-start(f32[40,8]{0,1:T(8,128)} %param.11) | copy-start | bytes 3844
  289.8 77.6 %all-to-all-start.1 = ((bf16[64,10,512]{2,1,0:T(8,128)(2,1)}), bf16[64,10,512]{2,1,0:T(8,128)(2,1)S(1)}, u32[]{:S(2)}, u32[]{:S(2)}) async-start(bf16[64,10,512]{2,1,0:T(8,128)(2,1)} %reshape.109), calls=%async_computation.1 | async-start | bytes 2097152 | tf_op jit(solution)/shard_map/all_to_all | solution.py:101
Sparse Core Ops, SparseCore 0:
  128.6 60.9 all-gather.2
